TPU v7x, 256 devices: a whole 4x4x8 slice. The times are simulated.
256 devices in a mesh: blk: 32 (over y_hi, z, core), col: 8 (over y_lo, x).
Axes of the slice: x: 4, y: 4 (y_hi: 2, y_lo: 2; y = y_hi * 2 + y_lo), z: 8, core: 2. Of those that a mesh axis runs over, the one named last changes fastest.
Arguments:
- a_blocks: float32 [32, 128, 384, 128], P('col', None, 'blk'), may hold values from -6 to 6
- a_mask: int32 [32, 384], P('col', 'blk'), may hold values 0 or 1
- b_blocks: float32 [384, 128, 32, 128], P('blk', None, 'col'), may hold values from -0.0546875 to 0.0546875
- b_mask: int32 [384, 32], P('blk', 'col'), may hold values 0 or 1
- c_mask: int32 [32, 32], P('blk', 'col'), may hold values 0 or 1
Outputs:
- product: float32 [32, 128, 32, 128], P('blk', None, 'col')
All inputs are finite; a program needn't handle non-finite values. No bound on the sum of `a_mask` or of `b_mask` or of `c_mask` on one device may be relied on, other than what follows from the above.
Results may differ from a plain program's by a relative error of at most 0.000071.
Values sent between devices are 32-bit elements; how exact they have to be, the bound alone decides.
No kernel may reach another device: no remote copies, remote signals or barrier semaphores. Data moves between devices by JAX's collectives and lax.ppermute only.
A program may use at most 128 MiB of HBM per device.

v0:
```python
import jax
import jax.numpy as jnp
from jax import lax
from jax.sharding import PartitionSpec as P


def shards(a_blocks, a_mask, b_blocks, b_mask, c_mask):
    masked_a = a_blocks * a_mask.astype(jnp.float32)[:, None, :, None]
    masked_b = b_blocks * b_mask.astype(jnp.float32)[:, None, :, None]
    col_count = masked_b.shape[2]
    block_side = masked_b.shape[3]
    flat_b = masked_b.reshape(masked_b.shape[0] * masked_b.shape[1], col_count * block_side)
    piece = lax.all_gather(masked_a, "col", axis=0, tiled=True)
    count = piece.shape[0]
    flat_piece = piece.reshape(count * piece.shape[1], piece.shape[2] * piece.shape[3])
    result = jnp.dot(
        flat_piece, flat_b, precision=lax.Precision.HIGHEST, preferred_element_type=jnp.float32
    )
    partial_value = result.reshape(count, piece.shape[1], col_count, block_side)
    owned = lax.psum_scatter(partial_value, "blk", scatter_dimension=0, tiled=True)
    return owned * c_mask.astype(jnp.float32)[:, None, :, None]


def solution(mesh):
    return jax.shard_map(
        shards,
        mesh=mesh,
        in_specs=(
            P("col", None, "blk", None),
            P("col", "blk"),
            P("blk", None, "col", None),
            P("blk", "col"),
            P("blk", "col"),
        ),
        out_specs=P("blk", None, "col", None),
        check_vma=False,
    )
```

profile of v0, /device:TPU:2, one launch (start us, length us, event | category | flops | bytes accessed | tf_op | source)
XLA Modules:
  0.0 535.6 jit_solution(895382643046142250)
XLA Ops:
  6.5 0.0 all-gather.2.cloned.1.call-start
  6.5 0.7 convert_element_type.9
  7.2 3.9 broadcast_multiply_fusion.1
  11.1 0.0 copy-start.2
  11.1 0.0 copy-start
  11.1 0.0 all-gather.2.cloned.1.call-update
  11.1 0.0 reduce-scatter.2.cloned.1.call-start
  11.2 0.6 copy-done.2
  11.8 0.1 copy.16
  11.9 1.1 copy-done
  13.0 0.7 broadcast_multiply_fusion
  13.7 0.3 copy.25
  14.1 2.3 copy.17
  16.4 0.0 copy-start.1
  16.4 247.4 %all-gather.2.cloned.1.call-done = f32[32,128,12,128]{3,1,2,0:T(8,128)} async-done(((f32[4,128,12,128]{3,1,2,0:T(8,128)}), f32[32,128,12,128]{3,1,2,0:T(8,128)}) %all-gather.2.cloned.1.call-update) | async-done | bytes 25165840 | tf_op jit(solution)/shard_map/all_gather | solution.py:13
  263.7 24.6 %copy.15 = f32[32,128,12,128]{1,3,2,0:T(8,128)} copy(f32[32,128,12,128]{3,1,2,0:T(8,128)} %all-gather.2.cloned.1.call-done) | data formatting | bytes 50331648 | tf_op jit(solution)/shard_map/all_gather | solution.py:13
  288.4 0.0 copy-done.1
  288.4 82.6 %fusion = f32[32,128,4,128]{3,1,2,0:T(8,128)} fusion(f32[32,128,1536,1]{1,2,3,0:T(8,128)} %bitcast.20, f32[4,128,1536,1]{2,1,0,3:T(8,128)S(1)} %bitcast.23), kind=kOutput, calls=%fused_computation.5 | convolution fusion | flops 38654705664 | bytes 36700160 | tf_op jit(solution)/shard_map/dot_general | solution.py:16
  371.0 0.0 copy-start.3
  371.0 0.0 reduce-scatter.2.cloned.1.call-update
  371.0 0.6 copy-done.3
  371.6 155.2 %reduce-scatter.2.cloned.1.call-done = f32[1,128,4,128]{3,1,2,0:T(8,128)} async-done(((f32[32,128,4,128]{3,1,2,0:T(8,128)}), f32[1,128,4,128]{3,1,2,0:T(8,128)}) %reduce-scatter.2.cloned.1.call-update) | async-done | bytes 262160 | tf_op jit(solution)/shard_map/reduce_scatter | solution.py:20
  526.8 1.0 broadcast_multiply_fusion.2
  527.9 0.9 copy.19
  (2 shorter events, 0.0 us)
Async XLA Ops:
  6.5 257.2 %all-gather.2.cloned.1.call-start = ((), (), s32[]{:S(2)}) async-start(), calls=%async_computation.1 | async-start | bytes 28311552 | tf_op jit(solution)/shard_map/all_gather | solution.py:13
  11.1 0.7 copy-start.2
  11.1 1.9 copy-start
  11.1 515.7 %reduce-scatter.2.cloned.1.call-start = ((), (), s32[]{:S(2)}) async-start(), calls=%async_computation.2 | async-start | bytes 8650752 | tf_op jit(solution)/shard_map/reduce_scatter | solution.py:20
  16.4 272.0 %copy-start.1 = (f32[512,1536]{1,0:T(8,128)S(1)}, f32[512,1536]{1,0:T(8,128)}, u32[]{:S(2)}) copy-start(f32[512,1536]{1,0:T(8,128)} %copy.17) | copy-start | bytes 9437188
  371.0 0.7 copy-start.3
Sparse Core Ops, SparseCore 0:
  11.3 252.4 all-gather.1
  371.1 155.6 reduce-scatter.1
where the time goes:
time: 536 us
  waiting for transfers between devices  403 us (75%)
  matrix products  82.6 us (15%)
  local copies, waits for them, and re-layouts  30.6 us (6%)
  between operations  13.4 us (2%)
  other arithmetic  6.34 us (1%)
    all_gather x1, waiting for transfers between devices, shards(): piece = lax.all_gather(masked_a, 'col', axis=0, tiled=True)  247 us
    reduce_scatter x1, waiting for transfers between devices, shards(): lax.psum_scatter(partial_value, 'blk', scatter_dimension=0, tiled=True)  155 us
    dot_general x1, matrix products, shards(): jnp.dot(flat_piece, flat_b, precision=lax.Precision.HIGHEST, preferred_el...  82.6 us
    all_gather x1, local copies, waits for them, and re-layouts, shards(): piece = lax.all_gather(masked_a, 'col', axis=0, tiled=True)  24.6 us
  transfers between devices with their start and end apart: 2, of which 2 were waited for; matrix products, arithmetic and copies ran while one was open for 1% of the time, Pallas kernels for 0%

commit v1 on v0

--- a/solution.py
+++ b/solution.py
@@ -10,7 +10,12 @@
     col_count = masked_b.shape[2]
     block_side = masked_b.shape[3]
     flat_b = masked_b.reshape(masked_b.shape[0] * masked_b.shape[1], col_count * block_side)
-    piece = lax.all_gather(masked_a, "col", axis=0, tiled=True)
+    piece = jnp.concatenate(
+        jax.lax.all_to_all(
+            jnp.stack([masked_a] * jax.lax.axis_size("col"), 0), "col", concat_axis=0, split_axis=0
+        ),
+        0,
+    )
     count = piece.shape[0]
     flat_piece = piece.reshape(count * piece.shape[1], piece.shape[2] * piece.shape[3])
     result = jnp.dot(

time: 536 us -> 658 us (1.23)
  waiting for transfers between devices: 403 us -> 528 us
  local copies, waits for them, and re-layouts: 30.6 us -> 18.1 us
  starting transfers between devices: 0.04 us -> 8.81 us
    all_to_all x0 -> x1, waiting for transfers between devices: none -> 366 us  [shards(): jax.lax.all_to_all(jnp.stack([masked_a] * jax.lax.axis_size('col'), 0), '...]
    all_gather x1 -> x0, waiting for transfers between devices: 247 us -> none  [shards(): piece = lax.all_gather(masked_a, 'col', axis=0, tiled=True)]
    all_gather x1 -> x0, local copies, waits for them, and re-layouts: 24.6 us -> none  [shards(): piece = lax.all_gather(masked_a, 'col', axis=0, tiled=True)]
    another operation x0 -> x1, local copies, waits for them, and re-layouts: none -> 11.5 us  [shards(): jnp.stack([masked_a] * jax.lax.axis_size('col'), 0)]
    all_to_all x0 -> x1, starting transfers between devices: none -> 8.81 us  [shards(): jax.lax.all_to_all(jnp.stack([masked_a] * jax.lax.axis_size('col'), 0), '...]
    reduce_scatter x1, waiting for transfers between devices: 155 us -> 162 us  [shards(): lax.psum_scatter(partial_value, 'blk', scatter_dimension=0, tiled=True)]
where the time goes in v1:
time: 658 us
  waiting for transfers between devices  528 us (80%)
  matrix products  83.5 us (13%)
  local copies, waits for them, and re-layouts  18.1 us (3%)
  between operations  13.4 us (2%)
  starting transfers between devices  8.81 us (1%)
    all_to_all x1, waiting for transfers between devices, shards(): jax.lax.all_to_all(jnp.stack([masked_a] * jax.lax.axis_size('col'), 0), '...  366 us
    reduce_scatter x1, waiting for transfers between devices, shards(): lax.psum_scatter(partial_value, 'blk', scatter_dimension=0, tiled=True)  162 us
    dot_general x1, matrix products, shards(): jnp.dot(flat_piece, flat_b, precision=lax.Precision.HIGHEST, preferred_el...  83.5 us
  transfers between devices with their start and end apart: 2, of which 2 were waited for; matrix products, arithmetic and copies ran while one was open for 1% of the time, Pallas kernels for 0%

profile of v1, /device:TPU:2, one launch (start us, length us, event | category | flops | bytes accessed | tf_op | source)
XLA Modules:
  0.0 658.0 jit_solution(3522056019874554176)
XLA Ops:
  6.5 0.7 convert_element_type.9
  7.2 3.8 broadcast_multiply_fusion.1
  11.0 2.4 copy.10
  13.4 11.5 %stack.2 = f32[8,4,128,12,128]{2,4,3,1,0:T(8,128)} broadcast(f32[4,128,12,128]{1,3,2,0:T(8,128)S(1)} %copy.10), dimensions={1,2,3,4} | broadcast | bytes 28311552 | tf_op jit(solution)/shard_map/stack | solution.py:15
  24.9 0.0 copy-start.1
  24.9 0.0 copy-start
  24.9 8.8 %all-to-all-start = ((f32[8,4,128,12,128]{2,4,3,1,0:T(8,128)}), f32[8,4,128,12,128]{2,4,3,1,0:T(8,128)}, u32[]{:S(2)}, u32[]{:S(2)}) async-start(f32[8,4,128,12,128]{2,4,3,1,0:T(8,128)} %stack.2), calls=%async_computation | async-start | bytes 50331648 | tf_op jit(solution)/shard_map/all_to_all | solution.py:14
  33.7 0.0 reduce-scatter.2.cloned.1.call-start
  33.7 0.0 copy-done.1
  33.7 0.1 copy.11
  33.8 0.0 copy-done
  33.8 0.7 broadcast_multiply_fusion
  34.6 0.3 copy.20
  34.9 2.3 copy.12
  37.2 365.7 %all-to-all-done = f32[8,4,128,12,128]{2,4,3,1,0:T(8,128)} async-done(((f32[8,4,128,12,128]{2,4,3,1,0:T(8,128)}), f32[8,4,128,12,128]{2,4,3,1,0:T(8,128)}, u32[]{:S(2)}, u32[]{:S(2)}) %all-to-all-start) | async-done | bytes 25165856 | tf_op jit(solution)/shard_map/all_to_all | solution.py:14
  402.9 83.5 %fusion = f32[32,128,4,128]{3,1,2,0:T(8,128)} fusion(f32[32,128,1536,1]{1,2,3,0:T(8,128)} %bitcast.7, f32[4,128,1536,1]{2,1,0,3:T(8,128)} %bitcast.22), kind=kOutput, calls=%fused_computation.5 | convolution fusion | flops 38654705664 | bytes 36700160 | tf_op jit(solution)/shard_map/dot_general | solution.py:21
  486.4 0.0 copy-start.2
  486.4 0.0 reduce-scatter.2.cloned.1.call-update
  486.4 0.6 copy-done.2
  487.1 162.1 %reduce-scatter.2.cloned.1.call-done = f32[1,128,4,128]{3,1,2,0:T(8,128)} async-done(((f32[32,128,4,128]{3,1,2,0:T(8,128)}), f32[1,128,4,128]{3,1,2,0:T(8,128)}) %reduce-scatter.2.cloned.1.call-update) | async-done | bytes 262160 | tf_op jit(solution)/shard_map/reduce_scatter | solution.py:25
  649.2 1.0 broadcast_multiply_fusion.2
  650.2 0.9 copy.14
  (2 shorter events, 0.0 us)
Async XLA Ops:
  24.9 8.8 %copy-start.1 = (s32[12,4]{0,1:T(4,128)S(1)}, s32[12,4]{0,1:T(4,128)}, u32[]{:S(2)}) copy-start(s32[12,4]{0,1:T(4,128)} %param.8) | copy-start | bytes 580
  24.9 8.9 %copy-start = (f32[12,128,4,128]{3,2,1,0:T(4,128)S(1)}, f32[12,128,4,128]{3,2,1,0:T(4,128)}, u32[]{:S(2)}) copy-start(f32[12,128,4,128]{3,2,1,0:T(4,128)} %param.7) | copy-start | bytes 9437188
  24.9 378.0 %all-to-all-start = ((f32[8,4,128,12,128]{2,4,3,1,0:T(8,128)}), f32[8,4,128,12,128]{2,4,3,1,0:T(8,128)}, u32[]{:S(2)}, u32[]{:S(2)}) async-start(f32[8,4,128,12,128]{2,4,3,1,0:T(8,128)} %stack.2), calls=%async_computation | async-start | bytes 50331648 | tf_op jit(solution)/shard_map/all_to_all | solution.py:14
  33.7 615.5 %reduce-scatter.2.cloned.1.call-start = ((), (), s32[]{:S(2)}) async-start(), calls=%async_computation.2 | async-start | bytes 8650752 | tf_op jit(solution)/shard_map/reduce_scatter | solution.py:25
  486.4 0.7 copy-start.2
Sparse Core Ops, SparseCore 0:
  486.6 162.5 reduce-scatter.1
